TPU v7x, 128 devices: a whole 4x4x4 slice. The times are simulated.
128 devices in a mesh: az: 16 (over x_hi, z, core), tm: 8 (over x_lo, y).
Axes of the slice: x: 4 (x_hi: 2, x_lo: 2; x = x_hi * 2 + x_lo), y: 4, z: 4, core: 2. Of those that a mesh axis runs over, the one named last changes fastest.
Arguments:
- pressure: bfloat16 [16, 64, 128, 4096], P(None, 'az', 'tm'), may hold values from -6 to 6
- offsets: int32 [128, 16], P('tm'), may hold values from -1 to 0
- frac: float32 [128, 16], P('tm'), may hold values from 0 to 1
Outputs:
- csm: float32 [256, 2, 1024, 1024], P('tm', None, 'az')
All inputs are finite; a program needn't handle non-finite values.
Results may differ from a plain program's by a relative error of at most 0.0065.
Values may be sent and summed in bfloat16 or wider, within the bound.
No kernel may reach another device: no remote copies, remote signals or barrier semaphores. Data moves between devices by JAX's collectives and lax.ppermute only.
A program may use at most 192 MiB of HBM per device.

v0:
```python
import math
import jax
import jax.numpy as jnp
from jax import lax
from jax.sharding import PartitionSpec as P

FREQS = 256


def extended(block, sides, width):
    for axis, dim in sides:
        count = lax.axis_size(axis)
        forward = [(i, i + 1) for i in range(count - 1)]
        forward.append((count - 1, 0))
        backward = [(target, source) for source, target in forward]
        low = lax.ppermute(
            lax.slice_in_dim(block, block.shape[dim] - width, None, axis=dim), axis, forward
        )
        high = lax.ppermute(lax.slice_in_dim(block, 0, width, axis=dim), axis, backward)
        block = jnp.concatenate([low, block, high], axis=dim)
    return block


def dft_table(length, freqs):
    times = jnp.arange(length, dtype=jnp.int32)
    bins = jnp.arange(1, freqs + 1, dtype=jnp.int32)
    phase = (times[:, None] * bins[None, :] % length).astype(jnp.float32) * (2.0 * math.pi / length)
    hann = 0.5 - 0.5 * jnp.cos(times.astype(jnp.float32) * (2.0 * math.pi / length))
    factor = hann[:, None] / math.sqrt(3.0 * length / 8.0)
    return jnp.concatenate([factor * jnp.cos(phase), -factor * jnp.sin(phase)], axis=1).astype(
        jnp.bfloat16
    )


def interp_weights(offsets, frac):
    rows = []
    for shift in range(-1, 2):
        low = (offsets == shift).astype(frac.dtype)
        high = (offsets + 1 == shift).astype(frac.dtype)
        rows.append((1.0 - frac) * low + frac * high)
    return jnp.stack(rows, 0)


def rotated_rows(rows):
    split = rows.reshape(rows.shape[0], rows.shape[1], rows.shape[2] // 2, 2)
    return jnp.stack([split[..., 1], -split[..., 0]], -1).reshape(rows.shape)


def cross_terms(rows, turned, columns):
    real = jnp.einsum("fqk,fpk->fqp", rows, columns, preferred_element_type=jnp.float32)
    imag = jnp.einsum("fqk,fpk->fqp", turned, columns, preferred_element_type=jnp.float32)
    return jnp.stack([real, imag], 1)


def shards(pressure, offsets, frac):
    cycles, sector, blocks, length = pressure.shape
    subs = offsets.shape[1]
    sub_len = length // subs
    padded = extended(pressure, (("az", 1),), 1)
    weights = interp_weights(offsets, frac)
    total = jnp.zeros((cycles, sector, blocks, subs, sub_len), jnp.float32)
    for shift in range(3):
        moved = padded[:, shift : shift + sector].reshape(cycles, sector, blocks, subs, sub_len)
        total = total + weights[shift][None, None, :, :, None] * moved
    virtual = total.astype(jnp.bfloat16).reshape(cycles * sector * blocks, length)
    table = dft_table(length, FREQS)
    freqs = table.shape[1] // 2
    spectra = jnp.dot(virtual, table, preferred_element_type=jnp.float32).astype(jnp.bfloat16)
    spectra = spectra.reshape(cycles, sector, blocks, 2, freqs).transpose(4, 1, 0, 2, 3)
    spectra = spectra.reshape(freqs, sector * cycles, blocks, 2)
    local_rows = sector * cycles
    gathered = lax.all_gather(spectra, "az", axis=1, tiled=True)
    shared = lax.all_to_all(gathered, "tm", split_axis=0, concat_axis=2, tiled=True)
    width = shared.shape[2]
    columns = shared.reshape(shared.shape[0], shared.shape[1], width * 2)
    start = lax.axis_index("az") * local_rows
    rows = lax.dynamic_slice_in_dim(columns, start, local_rows, 1)
    result = cross_terms(rows, rotated_rows(rows), columns)
    return result * (1.0 / width)


def solution(mesh):
    return jax.shard_map(
        shards,
        mesh=mesh,
        in_specs=(P(None, "az", "tm", None), P("tm", None), P("tm", None)),
        out_specs=P("tm", None, "az", None),
        check_vma=False,
    )
```

profile of v0, /device:TPU:1, one launch (start us, length us, event | category | flops | bytes accessed | tf_op | source)
XLA Modules:
  0.0 562.0 jit_solution(8039521140243428556)
XLA Ops:
  6.5 4.7 fusion.19
  11.3 3.0 collective-permute-start
  14.3 2.1 mul.142
  16.5 19.6 %copy.35 = f32[128,8,16,256]{3,1,2,0:T(8,128)} copy(f32[128,8,16,256]{3,2,1,0:T(8,128)S(1)} %bitcast.38) | data formatting | bytes 33554432
  36.1 2.1 mul.137
  38.2 19.0 %copy.34 = f32[128,8,16,256]{3,1,2,0:T(8,128)} copy(f32[128,8,16,256]{3,2,1,0:T(8,128)S(1)} %bitcast.39) | data formatting | bytes 33554432
  57.3 2.1 mul.132
  59.4 19.3 %copy.33 = f32[128,8,16,256]{3,1,2,0:T(8,128)} copy(f32[128,8,16,256]{3,2,1,0:T(8,128)S(1)} %bitcast.40) | data formatting | bytes 33554432
  78.8 19.2 %multiply_convert_fusion.1 = (bf16[4096,256]{1,0:T(8,128)(2,1)}, bf16[4096,256]{1,0:T(8,128)(2,1)}) fusion(s32[256]{0:T(256)S(1)} %iota_add_fusion, f32[4096]{0:T(1024)S(1)} %get-tuple-element.16, f32[4096]{0:T(1024)S(1)} %get-tuple-element.17), kind=kLoop, calls=%fused_computation.20 | loop fusion | flops 18874368 | bytes 4228096 | tf_op jit(solution)/shard_map/convert.3
  98.1 8.1 %pad_maximum_fusion.1 = (bf16[16,4,16,4096]{3,2,1,0:T(8,128)(2,1)}, bf16[16,4,16,4096]{3,2,1,0:T(8,128)(2,1)}) fusion(bf16[16,4,16,4096]{3,2,1,0:T(8,128)(2,1)S(1)} %bitcast.43, bf16[16,1,16,4096]{3,2,1,0:T(8,128)(2,1)} %collective-permute-done, bf16[16,1,16,4096]{3,2,1,0:T(8,128)(2,1)} %collective-permute-done.1), kind=kLoop, calls=%fused_computation.8 | loop fusion | flops 8388608 | bytes 29360128 | tf_op jit(solution)/shard_map/concatenate | solution.py:20
  106.2 26.0 %fusion.1 = bf16[1024,4096]{1,0:T(8,128)(2,1)} fusion(f32[1024,4096]{1,0:T(8,128)} %bitcast.35, f32[1024,4096]{1,0:T(8,128)} %bitcast.36, f32[1024,4096]{1,0:T(8,128)} %bitcast.37, bf16[16,4,16,4096]{3,2,1,0:T(8,128)(2,1)} %get-tuple-element.6, bf16[16,4,16,4096]{3,2,1,0:T(8,128)(2,1)S(1)} %bitcast.45, bf16[16,4,16,4096]{3,2,1,0:T(8,128)(2,1)} %get-tuple-element.5), kind=kLoop, calls=%fused_computation.3 | loop fusion | flops 37748736 | bytes 83886080 | tf_op jit(solution)/shard_map/convert_element_type | solution.py:65
  132.2 9.1 %fusion.14 = bf16[1024,512]{1,0:T(8,128)(2,1)S(1)} fusion(bf16[1024,4096]{1,0:T(8,128)(2,1)} %fusion.1, bf16[4096,256]{1,0:T(8,128)(2,1)} %get-tuple-element.15, bf16[4096,256]{1,0:T(8,128)(2,1)} %get-tuple-element.14), kind=kOutput, calls=%fused_computation.28 | convolution fusion | flops 4303880192 | bytes 13631488 | tf_op jit(solution)/shard_map/dot_general | solution.py:68
  142.9 111.5 %all-gather.2.cloned.1.call-done = bf16[256,1024,16,2]{0,2,3,1:T(8,128)(2,1)} async-done(((bf16[256,64,16,2]{0,2,3,1:T(8,128)(2,1)}), bf16[256,1024,16,2]{0,2,3,1:T(8,128)(2,1)}) %all-gather.2.cloned.1.call-update) | async-done | bytes 16777232 | tf_op jit(solution)/shard_map/all_gather | solution.py:72
  254.4 26.0 %copy.25 = bf16[256,1024,16,2]{1,2,3,0:T(8,128)(2,1)} copy(bf16[256,1024,16,2]{0,2,3,1:T(8,128)(2,1)} %all-gather.2.cloned.1.call-done) | data formatting | bytes 33554432 | tf_op jit(solution)/shard_map/all_gather | solution.py:72
  280.4 5.7 %all-to-all-start = ((bf16[256,1024,16,2]{1,2,3,0:T(8,128)(2,1)}), bf16[256,1024,16,2]{1,2,3,0:T(8,128)(2,1)}, u32[]{:S(2)}, u32[]{:S(2)}) async-start(bf16[256,1024,16,2]{1,2,3,0:T(8,128)(2,1)} %copy.25), calls=%async_computation | async-start | bytes 33554432 | tf_op jit(solution)/shard_map/all_to_all | solution.py:73
  286.1 183.5 %all-to-all-done = bf16[256,1024,16,2]{1,2,3,0:T(8,128)(2,1)} async-done(((bf16[256,1024,16,2]{1,2,3,0:T(8,128)(2,1)}), bf16[256,1024,16,2]{1,2,3,0:T(8,128)(2,1)}, u32[]{:S(2)}, u32[]{:S(2)}) %all-to-all-start) | async-done | bytes 16777248 | tf_op jit(solution)/shard_map/all_to_all | solution.py:73
  469.6 18.6 %copy.26 = bf16[32,1024,8,16,2]{1,0,4,3,2:T(8,128)(2,1)} copy(bf16[32,1024,8,16,2]{1,3,4,0,2:T(8,128)(2,1)} %bitcast.6) | data formatting | bytes 33554432 | tf_op jit(solution)/shard_map/all_to_all | solution.py:73
  488.3 23.2 %copy.27 = bf16[32,1024,256]{2,1,0:T(8,128)(2,1)} copy(bf16[32,1024,256]{1,0,2:T(8,128)(2,1)} %bitcast.41) | data formatting | bytes 33554432 | tf_op jit(solution)/shard_map/reshape | solution.py:75
  511.5 1.3 constant_dynamic-slice_fusion
  512.8 3.1 copy.29
  515.9 14.2 %convolution_bitcast_fusion = f32[32,1,64,1024]{3,2,0,1:T(8,128)} fusion(bf16[32,64,256]{2,1,0:T(8,128)(2,1)S(1)} %constant_dynamic-slice_fusion, bf16[32,1024,256]{2,1,0:T(8,128)(2,1)} %copy.27), kind=kOutput, calls=%fused_computation.24 | convolution fusion | flops 1073741824 | bytes 26214400 | tf_op jit(solution)/shard_map/fqk,fpk->fqp/dot_general | solution.py:50
  530.6 11.2 %convolution_bitcast_fusion.1 = f32[32,1,64,1024]{3,2,0,1:T(8,128)} fusion(bf16[32,1024,256]{2,1,0:T(8,128)(2,1)} %copy.27, bf16[32,64,256]{1,0,2:T(8,128)(2,1)S(1)} %bitcast.46), kind=kOutput, calls=%fused_computation.25 | convolution fusion | flops 1073741824 | bytes 26214400 | tf_op jit(solution)/shard_map/fqk,fpk->fqp/dot_general | solution.py:51
  541.9 6.8 %maximum_multiply_fusion = f32[32,2,64,1024]{3,2,0,1:T(8,128)S(1)} fusion(f32[32,1,64,1024]{3,2,0,1:T(8,128)} %convolution_bitcast_fusion.1, f32[32,1,64,1024]{3,2,0,1:T(8,128)} %convolution_bitcast_fusion), kind=kLoop, calls=%fused_computation | loop fusion | flops 8388608 | bytes 33554432 | tf_op jit(solution)/shard_map/mul | solution.py:79
  548.7 6.2 %copy.32 = f32[32,2,64,1024]{3,2,1,0:T(8,128)} copy(f32[32,2,64,1024]{3,2,0,1:T(8,128)S(1)} %maximum_multiply_fusion) | data formatting | bytes 33554432 | tf_op jit(solution)/shard_map/mul | solution.py:79
  (26 shorter events, 2.4 us)
Async XLA Ops:
  6.5 7.8 %copy-start = (f32[16,16]{1,0:T(8,128)S(1)}, f32[16,16]{1,0:T(8,128)}, u32[]{:S(2)}) copy-start(f32[16,16]{1,0:T(8,128)} %param.5) | copy-start | bytes 3076
  6.5 7.8 %copy-start.1 = (s32[16,16]{1,0:T(8,128)S(1)}, s32[16,16]{1,0:T(8,128)}, u32[]{:S(2)}) copy-start(s32[16,16]{1,0:T(8,128)} %param.4) | copy-start | bytes 3076
  6.5 247.9 %all-gather.2.cloned.1.call-start = ((), (), s32[]{:S(2)}) async-start(), calls=%async_computation.1 | async-start | bytes 17825792 | tf_op jit(solution)/shard_map/all_gather | solution.py:72
  11.3 86.8 %collective-permute-start = (bf16[16,1,16,4096]{3,2,1,0:T(8,128)(2,1)}, bf16[16,1,16,4096]{3,2,1,0:T(8,128)(2,1)}, u32[]{:S(2)}, u32[]{:S(2)}) collective-permute-start(bf16[16,1,16,4096]{3,2,1,0:T(8,128)(2,1)} %get-tuple-element.7), channel_id=1, source_target_pairs={{0,8},{8,16},{16,24},{24,32},{32,40},{40,48},{48,56},{56,64},{64,7... | collective-permute-start | bytes 6291464 | tf_op jit(solution)/shard_map/ppermute | solution.py:16
  14.3 83.8 %collective-permute-start.1 = (bf16[16,1,16,4096]{3,2,1,0:T(8,128)(2,1)}, bf16[16,1,16,4096]{3,2,1,0:T(8,128)(2,1)}, u32[]{:S(2)}, u32[]{:S(2)}) collective-permute-start(bf16[16,1,16,4096]{3,2,1,0:T(8,128)(2,1)} %get-tuple-element.8), channel_id=1, source_target_pairs={{8,0},{16,8},{24,16},{32,24},{40,32},{48,40},{56,48},{64,56},{72,6... | collective-permute-start | bytes 6291464 | tf_op jit(solution)/shard_map/ppermute | solution.py:19
  59.4 38.7 %slice-start = ((s8[8388608]{0:T(1024)(128)(4,1)}), s8[4194304]{0:T(1024)(128)(4,1)S(1)}, s32[]{:S(2)}) async-start(s8[8388608]{0:T(1024)(128)(4,1)} %bitcast.42), calls=%async_computation.2 | async-start | bytes 8388608
  59.4 38.6 %slice-start.1 = ((s8[8388608]{0:T(1024)(128)(4,1)}), s8[4194304]{0:T(1024)(128)(4,1)S(1)}, s32[]{:S(2)}) async-start(s8[8388608]{0:T(1024)(128)(4,1)} %bitcast.42), calls=%async_computation.3 | async-start | bytes 8388608
  78.8 27.3 %slice-start.2 = ((s8[8388608]{0:T(1024)(128)(4,1)}), s8[4194304]{0:T(1024)(128)(4,1)S(1)}, s32[]{:S(2)}) async-start(s8[8388608]{0:T(1024)(128)(4,1)} %bitcast.44), calls=%async_computation.4 | async-start | bytes 8388608
  98.0 8.1 %slice-start.3 = ((s8[8388608]{0:T(1024)(128)(4,1)}), s8[4194304]{0:T(1024)(128)(4,1)S(1)}, s32[]{:S(2)}) async-start(s8[8388608]{0:T(1024)(128)(4,1)} %bitcast.44), calls=%async_computation.5 | async-start | bytes 8388608
  280.4 189.2 %all-to-all-start = ((bf16[256,1024,16,2]{1,2,3,0:T(8,128)(2,1)}), bf16[256,1024,16,2]{1,2,3,0:T(8,128)(2,1)}, u32[]{:S(2)}, u32[]{:S(2)}) async-start(bf16[256,1024,16,2]{1,2,3,0:T(8,128)(2,1)} %copy.25), calls=%async_computation | async-start | bytes 33554432 | tf_op jit(solution)/shard_map/all_to_all | solution.py:73
Sparse Core Ops, SparseCore 0:
  143.1 111.2 all-gather.1
where the time goes:
time: 566 us; the launch traced here: 562 us
  waiting for transfers between devices  295 us (52%)
  local copies, waits for them, and re-layouts  149 us (26%)
  other arithmetic  60.8 us (11%)
  matrix products  34.5 us (6%)
  between operations  13.8 us (2%)
  starting transfers between devices  8.76 us (2%)
    all_to_all x1, waiting for transfers between devices, shards(): lax.all_to_all(gathered, 'tm', split_axis=0, concat_axis=2, tiled=True)  183 us
    all_gather x1, waiting for transfers between devices, shards(): gathered = lax.all_gather(spectra, 'az', axis=1, tiled=True)  111 us
    unnamed x15, local copies, waits for them, and re-layouts  58 us
    convert_element_type x1, other arithmetic, shards(): total.astype(jnp.bfloat16).reshape(cycles * sector * blocks, length)  26 us
    all_gather x1, local copies, waits for them, and re-layouts, shards(): gathered = lax.all_gather(spectra, 'az', axis=1, tiled=True)  26 us
    reshape x1, local copies, waits for them, and re-layouts, shards(): columns = shared.reshape(shared.shape[0], shared.shape[1], width * 2)  23.2 us
    another operation x1, other arithmetic  19.2 us
    all_to_all x1, local copies, waits for them, and re-layouts, shards(): lax.all_to_all(gathered, 'tm', split_axis=0, concat_axis=2, tiled=True)  18.6 us
  transfers between devices with their start and end apart: 4, of which 2 were waited for; matrix products, arithmetic and copies ran while one was open for 15% of the time, Pallas kernels for 0%

commit v1 on v0

--- a/solution.py
+++ b/solution.py
@@ -69,7 +69,9 @@
     spectra = spectra.reshape(cycles, sector, blocks, 2, freqs).transpose(4, 1, 0, 2, 3)
     spectra = spectra.reshape(freqs, sector * cycles, blocks, 2)
     local_rows = sector * cycles
-    gathered = lax.all_gather(spectra, "az", axis=1, tiled=True)
+    gathered = jnp.concatenate(
+        lax.all_to_all(jnp.stack([spectra] * lax.axis_size("az")), "az", 0, 0), axis=1
+    )
     shared = lax.all_to_all(gathered, "tm", split_axis=0, concat_axis=2, tiled=True)
     width = shared.shape[2]
     columns = shared.reshape(shared.shape[0], shared.shape[1], width * 2)

time: 566 us -> 636 us (1.12)
  blocking collectives: 0 us -> 193 us
  waiting for transfers between devices: 295 us -> 184 us
  between operations: 13.8 us -> 0.42 us
    all_to_all x0 -> x1, blocking collectives: none -> 193 us  [shards(): lax.all_to_all(jnp.stack([spectra] * lax.axis_size('az')), 'az', 0, 0)]
    all_gather x1 -> x0, waiting for transfers between devices: 111 us -> none  [shards(): gathered = lax.all_gather(spectra, 'az', axis=1, tiled=True)]
    reshape x0 -> x1, local copies, waits for them, and re-layouts: none -> 26 us  [shards(): jnp.concatenate(lax.all_to_all(jnp.stack([spectra] * lax.axis_size('az'))...]
    all_gather x1 -> x0, local copies, waits for them, and re-layouts: 26 us -> none  [shards(): gathered = lax.all_gather(spectra, 'az', axis=1, tiled=True)]
  transfers between devices with their start and end apart: 4 -> 3, of which waited for: 2 -> 1; matrix products, arithmetic and copies ran while one was open for 15% -> 13% of each run, Pallas kernels for 0% -> 0%
where the time goes in v1:
time: 636 us; the launch traced here: 632 us
  blocking collectives  193 us (30%)
  waiting for transfers between devices  184 us (29%)
  local copies, waits for them, and re-layouts  151 us (24%)
  other arithmetic  60.8 us (10%)
  matrix products  34.4 us (5%)
  starting transfers between devices  8.77 us (1%)
    all_to_all x1, blocking collectives, shards(): lax.all_to_all(jnp.stack([spectra] * lax.axis_size('az')), 'az', 0, 0)  193 us
    all_to_all x1, waiting for transfers between devices, shards(): lax.all_to_all(gathered, 'tm', split_axis=0, concat_axis=2, tiled=True)  184 us
    unnamed x15, local copies, waits for them, and re-layouts  58 us
    convert_element_type x1, other arithmetic, shards(): total.astype(jnp.bfloat16).reshape(cycles * sector * blocks, length)  26 us
    reshape x1, local copies, waits for them, and re-layouts, shards(): jnp.concatenate(lax.all_to_all(jnp.stack([spectra] * lax.axis_size('az'))...  26 us
    reshape x1, local copies, waits for them, and re-layouts, shards(): columns = shared.reshape(shared.shape[0], shared.shape[1], width * 2)  23.2 us
    another operation x1, other arithmetic  19.2 us
    all_to_all x1, local copies, waits for them, and re-layouts, shards(): lax.all_to_all(gathered, 'tm', split_axis=0, concat_axis=2, tiled=True)  18.6 us
  transfers between devices with their start and end apart: 3, of which 1 were waited for; matrix products, arithmetic and copies ran while one was open for 13% of the time, Pallas kernels for 0%

profile of v1, /device:TPU:1, one launch (start us, length us, event | category | flops | bytes accessed | tf_op | source)
XLA Modules:
  0.0 632.0 jit_solution(5746003530437398540)
XLA Ops:
  0.0 4.7 fusion.19
  4.7 3.0 collective-permute-start
  7.8 2.1 mul.142
  9.9 19.6 %copy.35 = f32[128,8,16,256]{3,1,2,0:T(8,128)} copy(f32[128,8,16,256]{3,2,1,0:T(8,128)S(1)} %bitcast.41) | data formatting | bytes 33554432
  29.5 2.1 mul.137
  31.7 19.0 %copy.34 = f32[128,8,16,256]{3,1,2,0:T(8,128)} copy(f32[128,8,16,256]{3,2,1,0:T(8,128)S(1)} %bitcast.42) | data formatting | bytes 33554432
  50.7 2.1 mul.132
  52.9 19.3 %copy.33 = f32[128,8,16,256]{3,1,2,0:T(8,128)} copy(f32[128,8,16,256]{3,2,1,0:T(8,128)S(1)} %bitcast.43) | data formatting | bytes 33554432
  72.3 19.2 %multiply_convert_fusion.1 = (bf16[4096,256]{1,0:T(8,128)(2,1)}, bf16[4096,256]{1,0:T(8,128)(2,1)}) fusion(s32[256]{0:T(256)S(1)} %iota_add_fusion, f32[4096]{0:T(1024)S(1)} %get-tuple-element.16, f32[4096]{0:T(1024)S(1)} %get-tuple-element.17), kind=kLoop, calls=%fused_computation.20 | loop fusion | flops 18874368 | bytes 4228096 | tf_op jit(solution)/shard_map/convert.3
  91.5 8.1 %pad_maximum_fusion.1 = (bf16[16,4,16,4096]{3,2,1,0:T(8,128)(2,1)}, bf16[16,4,16,4096]{3,2,1,0:T(8,128)(2,1)}) fusion(bf16[16,4,16,4096]{3,2,1,0:T(8,128)(2,1)S(1)} %bitcast.47, bf16[16,1,16,4096]{3,2,1,0:T(8,128)(2,1)} %collective-permute-done, bf16[16,1,16,4096]{3,2,1,0:T(8,128)(2,1)} %collective-permute-done.1), kind=kLoop, calls=%fused_computation.8 | loop fusion | flops 8388608 | bytes 29360128 | tf_op jit(solution)/shard_map/concatenate | solution.py:20
  99.7 26.0 %fusion.1 = bf16[1024,4096]{1,0:T(8,128)(2,1)} fusion(f32[1024,4096]{1,0:T(8,128)} %bitcast.38, f32[1024,4096]{1,0:T(8,128)} %bitcast.39, f32[1024,4096]{1,0:T(8,128)} %bitcast.40, bf16[16,4,16,4096]{3,2,1,0:T(8,128)(2,1)} %get-tuple-element.6, bf16[16,4,16,4096]{3,2,1,0:T(8,128)(2,1)S(1)} %bitcast.49, bf16[16,4,16,4096]{3,2,1,0:T(8,128)(2,1)} %get-tuple-element.5), kind=kLoop, calls=%fused_computation.3 | loop fusion | flops 37748736 | bytes 83886080 | tf_op jit(solution)/shard_map/convert_element_type | solution.py:65
  125.7 9.1 %fusion.14 = bf16[1024,512]{1,0:T(8,128)(2,1)S(1)} fusion(bf16[1024,4096]{1,0:T(8,128)(2,1)} %fusion.1, bf16[4096,256]{1,0:T(8,128)(2,1)} %get-tuple-element.15, bf16[4096,256]{1,0:T(8,128)(2,1)} %get-tuple-element.14), kind=kOutput, calls=%fused_computation.28 | convolution fusion | flops 4303880192 | bytes 13631488 | tf_op jit(solution)/shard_map/dot_general | solution.py:68
  135.4 2.2 stack.16
  137.6 193.3 %all_to_all.20 = bf16[16,256,64,16,2]{1,3,4,2,0:T(8,128)(2,1)} all-to-all(bf16[16,256,64,16,2]{1,3,4,2,0:T(8,128)(2,1)S(1)} %stack.16), channel_id=1, replica_groups=mesh['az'=16,'tm'=8] {'az'}, dimensions={0} | all-to-all | bytes 33554432 | tf_op jit(solution)/shard_map/all_to_all | solution.py:73
  331.0 26.0 %copy.25 = bf16[256,1024,16,2]{1,2,3,0:T(8,128)(2,1)} copy(bf16[256,1024,16,2]{0,2,3,1:T(8,128)(2,1)} %bitcast.44) | data formatting | bytes 33554432 | tf_op jit(solution)/shard_map/reshape | solution.py:72
  356.9 5.8 all-to-all-start.1
  362.7 183.7 %all-to-all-done.1 = bf16[256,1024,16,2]{1,2,3,0:T(8,128)(2,1)} async-done(((bf16[256,1024,16,2]{1,2,3,0:T(8,128)(2,1)}), bf16[256,1024,16,2]{1,2,3,0:T(8,128)(2,1)}, u32[]{:S(2)}, u32[]{:S(2)}) %all-to-all-start.1) | async-done | bytes 16777248 | tf_op jit(solution)/shard_map/all_to_all | solution.py:75
  546.4 18.6 %copy.26 = bf16[32,1024,8,16,2]{1,0,4,3,2:T(8,128)(2,1)} copy(bf16[32,1024,8,16,2]{1,3,4,0,2:T(8,128)(2,1)} %bitcast.8) | data formatting | bytes 33554432 | tf_op jit(solution)/shard_map/all_to_all | solution.py:75
  565.1 23.2 %copy.27 = bf16[32,1024,256]{2,1,0:T(8,128)(2,1)} copy(bf16[32,1024,256]{1,0,2:T(8,128)(2,1)} %bitcast.45) | data formatting | bytes 33554432 | tf_op jit(solution)/shard_map/reshape | solution.py:77
  589.6 3.1 copy.29
  592.7 14.1 %convolution_bitcast_fusion = f32[32,1,64,1024]{3,2,0,1:T(8,128)} fusion(bf16[32,64,256]{2,1,0:T(8,128)(2,1)S(1)} %constant_dynamic-slice_fusion, bf16[32,1024,256]{2,1,0:T(8,128)(2,1)} %copy.27), kind=kOutput, calls=%fused_computation.24 | convolution fusion | flops 1073741824 | bytes 26214400 | tf_op jit(solution)/shard_map/fqk,fpk->fqp/dot_general | solution.py:50
  607.5 11.2 %convolution_bitcast_fusion.1 = f32[32,1,64,1024]{3,2,0,1:T(8,128)} fusion(bf16[32,1024,256]{2,1,0:T(8,128)(2,1)} %copy.27, bf16[32,64,256]{1,0,2:T(8,128)(2,1)S(1)} %bitcast.50), kind=kOutput, calls=%fused_computation.25 | convolution fusion | flops 1073741824 | bytes 26214400 | tf_op jit(solution)/shard_map/fqk,fpk->fqp/dot_general | solution.py:51
  618.7 6.8 %maximum_multiply_fusion = f32[32,2,64,1024]{3,2,0,1:T(8,128)S(1)} fusion(f32[32,1,64,1024]{3,2,0,1:T(8,128)} %convolution_bitcast_fusion.1, f32[32,1,64,1024]{3,2,0,1:T(8,128)} %convolution_bitcast_fusion), kind=kLoop, calls=%fused_computation | loop fusion | flops 8388608 | bytes 33554432 | tf_op jit(solution)/shard_map/mul | solution.py:81
  625.6 6.2 copy.32
  (25 shorter events, 2.7 us)
Async XLA Ops:
  0.0 7.8 %copy-start = (f32[16,16]{1,0:T(8,128)S(1)}, f32[16,16]{1,0:T(8,128)}, u32[]{:S(2)}) copy-start(f32[16,16]{1,0:T(8,128)} %param.5) | copy-start | bytes 3076
  0.0 7.8 %copy-start.1 = (s32[16,16]{1,0:T(8,128)S(1)}, s32[16,16]{1,0:T(8,128)}, u32[]{:S(2)}) copy-start(s32[16,16]{1,0:T(8,128)} %param.4) | copy-start | bytes 3076
  4.7 86.8 %collective-permute-start = (bf16[16,1,16,4096]{3,2,1,0:T(8,128)(2,1)}, bf16[16,1,16,4096]{3,2,1,0:T(8,128)(2,1)}, u32[]{:S(2)}, u32[]{:S(2)}) collective-permute-start(bf16[16,1,16,4096]{3,2,1,0:T(8,128)(2,1)} %get-tuple-element.7), channel_id=1, source_target_pairs={{0,8},{8,16},{16,24},{24,32},{32,40},{40,48},{48,56},{56,64},{64,7... | collective-permute-start | bytes 6291464 | tf_op jit(solution)/shard_map/ppermute | solution.py:16
  7.8 83.8 %collective-permute-start.1 = (bf16[16,1,16,4096]{3,2,1,0:T(8,128)(2,1)}, bf16[16,1,16,4096]{3,2,1,0:T(8,128)(2,1)}, u32[]{:S(2)}, u32[]{:S(2)}) collective-permute-start(bf16[16,1,16,4096]{3,2,1,0:T(8,128)(2,1)} %get-tuple-element.8), channel_id=1, source_target_pairs={{8,0},{16,8},{24,16},{32,24},{40,32},{48,40},{56,48},{64,56},{72,6... | collective-permute-start | bytes 6291464 | tf_op jit(solution)/shard_map/ppermute | solution.py:19
  52.9 38.7 %slice-start = ((s8[8388608]{0:T(1024)(128)(4,1)}), s8[4194304]{0:T(1024)(128)(4,1)S(1)}, s32[]{:S(2)}) async-start(s8[8388608]{0:T(1024)(128)(4,1)} %bitcast.46), calls=%async_computation.2 | async-start | bytes 8388608
  52.9 38.7 %slice-start.1 = ((s8[8388608]{0:T(1024)(128)(4,1)}), s8[4194304]{0:T(1024)(128)(4,1)S(1)}, s32[]{:S(2)}) async-start(s8[8388608]{0:T(1024)(128)(4,1)} %bitcast.46), calls=%async_computation.3 | async-start | bytes 8388608
  72.3 27.4 %slice-start.2 = ((s8[8388608]{0:T(1024)(128)(4,1)}), s8[4194304]{0:T(1024)(128)(4,1)S(1)}, s32[]{:S(2)}) async-start(s8[8388608]{0:T(1024)(128)(4,1)} %bitcast.48), calls=%async_computation.4 | async-start | bytes 8388608
  91.5 8.2 %slice-start.3 = ((s8[8388608]{0:T(1024)(128)(4,1)}), s8[4194304]{0:T(1024)(128)(4,1)S(1)}, s32[]{:S(2)}) async-start(s8[8388608]{0:T(1024)(128)(4,1)} %bitcast.48), calls=%async_computation.5 | async-start | bytes 8388608
  356.9 189.5 %all-to-all-start.1 = ((bf16[256,1024,16,2]{1,2,3,0:T(8,128)(2,1)}), bf16[256,1024,16,2]{1,2,3,0:T(8,128)(2,1)}, u32[]{:S(2)}, u32[]{:S(2)}) async-start(bf16[256,1024,16,2]{1,2,3,0:T(8,128)(2,1)} %copy.25), calls=%async_computation.1 | async-start | bytes 33554432 | tf_op jit(solution)/shard_map/all_to_all | solution.py:75
